TPU v7x, 32 devices: a whole 2x2x4 slice. The times are simulated.
32 devices in a mesh: groups: 2 (over x), height: 16 (over z, y, core).
Axes of the slice: x: 2, y: 2, z: 4, core: 2. Of those that a mesh axis runs over, the one named last changes fastest.
Arguments:
- latent: bfloat16 [3, 64, 80, 512], P(None, ('groups', 'height')), parts along dimension 1, may hold values from -120 to 120
- gain_first: float32 [512], replicated, may hold values from 0.1 to 1.9
- shift_first: float32 [512], replicated, may hold values from -3 to 3
- kernel_first: bfloat16 [27, 512, 512], P(None, 'height'), may hold values from -0.0546875 to 0.0546875
- bias_first: float32 [512], replicated, may hold values from -2 to 2
- gain_second: float32 [512], replicated, may hold values from 0.1 to 1.9
- shift_second: float32 [512], replicated, may hold values from -3 to 3
- kernel_second: bfloat16 [27, 512, 512], P(None, 'height'), may hold values from -0.0546875 to 0.0546875
- bias_second: float32 [512], replicated, may hold values from -2 to 2
Outputs:
- upsampled: bfloat16 [3, 128, 160, 512], P(None, ('groups', 'height')), parts along dimension 1
There are 2 independent parts, one for each index of `groups`. A program takes and returns all parts, laid end to end along the dimension named above; an argument that names none is the same for every part. Nothing has to cross between parts.
All inputs are finite; a program needn't handle non-finite values.
Results may differ from a plain program's by a relative error of at most 0.0045.
Values may be sent and summed in bfloat16 or wider, within the bound.
No kernel may reach another device: no remote copies, remote signals or barrier semaphores. Data moves between devices by JAX's collectives and lax.ppermute only.
A program may use at most 128 MiB of HBM per device.

v0:
```python
import jax
import jax.numpy as jnp
from jax import lax
from jax.sharding import PartitionSpec as P

GROUPS = 32


def with_halo(cells, sides, width):
    for axis, dim in sides:
        count = lax.axis_size(axis)
        ends = count - 1
        head = lax.slice_in_dim(cells, 0, width, axis=dim)
        tail = lax.slice_in_dim(cells, cells.shape[dim] - width, cells.shape[dim], axis=dim)
        cells = jnp.concatenate(
            [
                lax.ppermute(tail, axis, [(i, (i + 1) % count) for i in range(ends)]),
                cells,
                lax.ppermute(head, axis, [((i + 1) % count, i) for i in range(ends)]),
            ],
            axis=dim,
        )
    return cells


def moments(field, cells):
    values = field.astype(jnp.float32)
    chan_total = values.shape[3]
    group_size = chan_total // GROUPS
    chan_sums = jnp.sum(values, axis=(0, 1, 2)).reshape(GROUPS, group_size).sum(axis=1)
    squares = jnp.sum(values * values, axis=(0, 1, 2)).reshape(GROUPS, group_size).sum(axis=1)
    summed, spread = lax.psum((chan_sums, squares), "height")
    group_mean = summed / cells
    variance = spread / cells - group_mean * group_mean
    mean_chan = jnp.repeat(group_mean, group_size)
    scale_chan = jnp.repeat(lax.rsqrt(variance + 1e-06), group_size)
    return (mean_chan, scale_chan)


def activate(field, mean_chan, scale_chan, norm_gain, norm_shift):
    values = field.astype(jnp.float32)
    normed = (values - mean_chan) * scale_chan * norm_gain + norm_shift
    return jax.nn.silu(normed).astype(jnp.bfloat16)


def pad_local(extended):
    leading = jnp.concatenate([extended[:1], extended[:1], extended], axis=0)
    return jnp.pad(leading, ((0, 0), (0, 0), (1, 1), (0, 0)))


def tap_sum(padded, kernel_part, out_rows):
    frame_total = padded.shape[0] - 2
    col_total = padded.shape[2] - 2
    summed = jnp.zeros((frame_total, out_rows, col_total, kernel_part.shape[2]), jnp.float32)
    for step_t in range(3):
        for step_h in range(3):
            for step_w in range(3):
                window = padded[
                    step_t : step_t + frame_total,
                    step_h : step_h + out_rows,
                    step_w : step_w + col_total,
                ]
                summed = summed + jnp.einsum(
                    "fhwk,ko->fhwo",
                    window,
                    kernel_part[9 * step_t + 3 * step_h + step_w],
                    preferred_element_type=jnp.float32,
                )
    return summed


def convolve(padded, kernel, out_rows):
    gathered = lax.all_gather(kernel, "height", axis=1, tiled=True)
    return tap_sum(padded, gathered, out_rows)


def per_device(
    latent,
    gain_first,
    shift_first,
    kernel_first,
    bias_first,
    gain_second,
    shift_second,
    kernel_second,
    bias_second,
):
    frame_total, slab_rows, col_total, chan_total = latent.shape
    slab_count = lax.axis_size("height")
    cells = float(frame_total * slab_rows * slab_count * col_total * (chan_total // GROUPS))
    mean_chan, scale_chan = moments(latent, cells)
    act_first = activate(latent, mean_chan, scale_chan, gain_first, shift_first)
    extended = with_halo(act_first, (("height", 1),), 1)
    hidden = (convolve(pad_local(extended), kernel_first, slab_rows) + bias_first).astype(
        jnp.bfloat16
    )
    mean_next, scale_next = moments(hidden, cells)
    act_second = activate(hidden, mean_next, scale_next, gain_second, shift_second)
    extended_next = with_halo(act_second, (("height", 1),), 1)
    branch = convolve(pad_local(extended_next), kernel_second, slab_rows) + bias_second
    summed = (latent.astype(jnp.float32) + branch).astype(jnp.bfloat16)
    return jnp.repeat(jnp.repeat(summed, 2, axis=1), 2, axis=2)


def solution(mesh):
    placed = (
        P(None, ("groups", "height"), None, None),
        P(),
        P(),
        P(None, "height", None),
        P(),
        P(),
        P(),
        P(None, "height", None),
        P(),
    )
    return jax.shard_map(
        per_device,
        mesh=mesh,
        in_specs=placed,
        out_specs=P(None, ("groups", "height"), None, None),
        check_vma=False,
    )
```

profile of v0, /device:TPU:0, one launch (start us, length us, event | category | flops | bytes accessed | tf_op | source)
XLA Modules:
  0.0 292.4 jit_solution(4379032982951424562)
XLA Ops:
  8.6 36.1 %all-reduce.3 = (f32[32]{0:T(128)S(1)}, f32[32]{0:T(128)S(1)}) all-reduce(f32[32]{0:T(128)S(1)} %reduce_sum.75, f32[32]{0:T(128)S(1)} %reduce_sum.73), channel_id=1, replica_groups=mesh['groups'=2,'height'=16] {'height'}, use_global_device_ids=true, to_apply=%region_5.0 | all-reduce | flops 64 | bytes 512 | tf_op jit(solution)/shard_map/psum | solution.py:32
  48.0 2.1 collective-permute-done.1
  50.3 75.3 %all-gather.3.cloned.1.call-done = bf16[27,512,512]{2,1,0:T(8,128)(2,1)} async-done(((bf16[27,32,512]{2,1,0:T(8,128)(2,1)}), bf16[27,512,512]{2,1,0:T(8,128)(2,1)}) %all-gather.3.cloned.1.call-update) | async-done | bytes 14155792 | tf_op jit(solution)/shard_map/all_gather | solution.py:73
  125.7 2.6 fusion.77
  128.2 3.2 %fusion.80 = f32[3,2,80,512]{3,2,1,0:T(8,128)} fusion(bf16[27,512,512]{2,1,0:T(8,128)(2,1)} %all-gather.3.cloned.1.call-done, bf16[3,1,80,512]{3,2,1,0:T(8,128)(2,1)S(1)} %collective-permute-done.1, bf16[3,2,80,512]{3,2,1,0:T(8,128)(2,1)S(1)} %fusion.28, bf16[3,1,80,512]{3,2,1,0:T(8,128)(2,1)S(1)} %collective-permute-done, ...), kind=kOutput, calls=%fused_computation.134 | convolution fusion | flops 256901120 | bytes 2818048 | tf_op jit(solution)/shard_map/fhwk,ko->fhwo/dot_general | solution.py:63
  131.5 2.4 fusion.83
  133.9 1.5 fusion.71
  140.2 1.4 fusion.85
  141.6 1.4 fusion.87
  143.0 1.4 fusion.88
  144.4 1.4 fusion.90
  152.7 1.4 fusion.72
  154.1 1.4 fusion.86
  156.9 1.4 fusion.92
  158.3 6.9 %convert_reduce_fusion.1 = (f32[512]{0:T(512)S(1)}, f32[512]{0:T(512)S(1)}, bf16[3,2,80,512]{3,2,1,0:T(8,128)(2,1)S(1)}) fusion(f32[512]{0:T(512)S(1)} %copy-done.4, f32[3,2,80,512]{3,2,1,0:T(8,128)} %fusion.70, f32[3,2,80,512]{3,2,1,0:T(8,128)} %fusion.34, f32[3,2,80,512]{3,2,1,0:T(8,128)S(1)} %fusion.71, bf16[27,512,512]{2,1,0:T(8,128)(2,1)S(1)} %copy-done.1, ...), kind=kOutput, calls=%fused_computation.8 | convolution fusion | flops 259521536 | bytes 28219392 | tf_op jit(solution)/shard_map/fhwk,ko->fhwo/dot_general | solution.py:63
  165.7 31.7 %all-reduce.2 = (f32[32]{0:T(128)S(1)}, f32[32]{0:T(128)S(1)}) all-reduce(f32[32]{0:T(128)S(1)} %reduce_sum.79, f32[32]{0:T(128)S(1)} %reduce_sum.77), channel_id=1, replica_groups=mesh['groups'=2,'height'=16] {'height'}, use_global_device_ids=true, to_apply=%region_11.12 | all-reduce | flops 64 | bytes 512 | tf_op jit(solution)/shard_map/psum | solution.py:32
  199.4 1.5 collective-permute-start.3
  200.9 41.7 %all-gather.5.cloned.1.call-done = bf16[27,512,512]{2,1,0:T(8,128)(2,1)} async-done(((bf16[27,32,512]{2,1,0:T(8,128)(2,1)}), bf16[27,512,512]{2,1,0:T(8,128)(2,1)}) %all-gather.5.cloned.1.call-update) | async-done | bytes 14155792 | tf_op jit(solution)/shard_map/all_gather | solution.py:73
  242.6 1.6 fusion.48
  244.2 2.8 fusion.59
  247.1 2.6 fusion.56
  249.7 2.4 fusion.53
  252.1 1.4 fusion.38
  259.4 1.4 fusion.61
  263.5 1.4 fusion.64
  264.9 1.4 fusion.65
  267.7 1.5 fusion.67
  269.2 1.4 fusion.68
  270.6 1.4 fusion.69
  273.4 7.4 %fusion.8 = bf16[3,2,80,512]{3,2,1,0:T(8,128)(2,1)} fusion(f32[3,2,80,512]{3,2,1,0:T(8,128)} %fusion.46, f32[3,2,80,512]{3,2,1,0:T(8,128)} %fusion.42, f32[3,2,80,512]{3,2,1,0:T(8,128)S(1)} %fusion.47, bf16[3,2,80,512]{3,2,1,0:T(8,128)(2,1)S(1)} %copy-done.2, f32[3,2,80,512]{3,2,1,0:T(8,128)S(1)} %fusion.48, f32[3,2,80,512]{3,2,1,0:T(8,128)S(1)} %fusion.49, ...), kind=kOutput, calls=%fused_computation.21 | convolution fusion | flops 259031040 | bytes 28706816 | tf_op jit(solution)/shard_map/fhwk,ko->fhwo/dot_general | solution.py:63
  281.9 1.4 broadcast_in_dim.29
  283.4 2.2 reshape.33
  (88 shorter events, 33.5 us)
Async XLA Ops:
  6.5 1.5 copy-start.2
  6.5 38.4 %copy-start.7 = (f32[512]{0:T(512)S(1)}, f32[512]{0:T(512)}, u32[]{:S(2)}) copy-start(f32[512]{0:T(512)} %param.10) | copy-start | bytes 6148
  6.5 38.5 %copy-start.6 = (f32[512]{0:T(512)S(1)}, f32[512]{0:T(512)}, u32[]{:S(2)}) copy-start(f32[512]{0:T(512)} %param.11) | copy-start | bytes 6148
  6.5 119.1 %all-gather.3.cloned.1.call-start = ((), (), s32[]{:S(2)}) async-start(), calls=%async_computation | async-start | bytes 15040512 | tf_op jit(solution)/shard_map/all_gather | solution.py:73
  7.3 235.3 %all-gather.5.cloned.1.call-start = ((), (), s32[]{:S(2)}) async-start(), calls=%async_computation.1 | async-start | bytes 15040512 | tf_op jit(solution)/shard_map/all_gather | solution.py:73
  45.4 2.6 collective-permute-start
  46.7 3.4 %collective-permute-start.1 = (bf16[3,1,80,512]{3,2,1,0:T(8,128)(2,1)S(1)}, bf16[3,1,80,512]{3,2,1,0:T(8,128)(2,1)S(1)}, u32[]{:S(2)}, u32[]{:S(2)}) collective-permute-start(bf16[3,1,80,512]{3,2,1,0:T(8,128)(2,1)S(1)} %get-tuple-element.16), channel_id=1, source_target_pairs={{1,0},{2,1},{3,2},{4,3},{5,4},{6,5},{7,6},{8,7},{9,8},{10,9},{11,1... | collective-permute-start | bytes 737288 | tf_op jit(solution)/shard_map/ppermute | solution.py:19
  125.7 9.7 %copy-start.1 = (bf16[27,512,512]{2,1,0:T(8,128)(2,1)S(1)}, bf16[27,512,512]{2,1,0:T(8,128)(2,1)}, u32[]{:S(2)}) copy-start(bf16[27,512,512]{2,1,0:T(8,128)(2,1)} %all-gather.3.cloned.1.call-done) | copy-start | bytes 42467332
  155.5 2.8 copy-start.3
  155.5 2.8 copy-start.4
  158.3 39.4 %copy-start.8 = (f32[512]{0:T(512)S(1)}, f32[512]{0:T(512)}, u32[]{:S(2)}) copy-start(f32[512]{0:T(512)} %param.15) | copy-start | bytes 6148
  158.3 39.4 %copy-start.9 = (f32[512]{0:T(512)S(1)}, f32[512]{0:T(512)}, u32[]{:S(2)}) copy-start(f32[512]{0:T(512)} %param.14) | copy-start | bytes 6148
  198.1 46.1 %collective-permute-start.2 = (bf16[3,1,80,512]{3,2,1,0:T(8,128)(2,1)S(1)}, bf16[3,1,80,512]{3,2,1,0:T(8,128)(2,1)S(1)}, u32[]{:S(2)}, u32[]{:S(2)}) collective-permute-start(bf16[3,1,80,512]{3,2,1,0:T(8,128)(2,1)S(1)} %get-tuple-element.13), channel_id=1, source_target_pairs={{0,1},{1,2},{2,3},{3,4},{4,5},{5,6},{6,7},{7,8},{8,9},{9,10},{10,1... | collective-permute-start | bytes 737288 | tf_op jit(solution)/shard_map/ppermute | solution.py:17
  199.4 44.8 %collective-permute-start.3 = (bf16[3,1,80,512]{3,2,1,0:T(8,128)(2,1)S(1)}, bf16[3,1,80,512]{3,2,1,0:T(8,128)(2,1)S(1)}, u32[]{:S(2)}, u32[]{:S(2)}) collective-permute-start(bf16[3,1,80,512]{3,2,1,0:T(8,128)(2,1)S(1)} %get-tuple-element.14), channel_id=1, source_target_pairs={{1,0},{2,1},{3,2},{4,3},{5,4},{6,5},{7,6},{8,7},{9,8},{10,9},{11,1... | collective-permute-start | bytes 737288 | tf_op jit(solution)/shard_map/ppermute | solution.py:19
  242.6 9.6 %copy-start = (bf16[27,512,512]{2,1,0:T(8,128)(2,1)S(1)}, bf16[27,512,512]{2,1,0:T(8,128)(2,1)}, u32[]{:S(2)}) copy-start(bf16[27,512,512]{2,1,0:T(8,128)(2,1)} %all-gather.5.cloned.1.call-done) | copy-start | bytes 42467332
  272.0 1.4 copy-start.5
Sparse Core Ops, SparseCore 0:
  9.5 116.0 all-gather.2
  127.9 114.6 all-gather.4
where the time goes:
time: 293 us; the launch traced here: 292 us
  waiting for transfers between devices  121 us (41%)
  matrix products  77.5 us (26%)
  blocking collectives  67.8 us (23%)
  between operations  13.7 us (5%)
  local copies, waits for them, and re-layouts  5.75 us (2%)
  starting transfers between devices  5.41 us (2%)
    all_gather x2, waiting for transfers between devices, convolve(): gathered = lax.all_gather(kernel, 'height', axis=1, tiled=True)  117 us
    dot_general x54, matrix products, tap_sum(): jnp.einsum('fhwk,ko->fhwo', window, kernel_part[9 * step_t + 3 * step_h +...  77.5 us
    psum x2, blocking collectives, moments(): summed, spread = lax.psum((chan_sums, squares), 'height')  67.8 us
  transfers between devices with their start and end apart: 6, of which 3 were waited for; matrix products, arithmetic and copies ran while one was open for 15% of the time, Pallas kernels for 0%

commit v1 on v0

--- a/solution.py
+++ b/solution.py
@@ -70,7 +70,21 @@
 
 
 def convolve(padded, kernel, out_rows):
-    gathered = lax.all_gather(kernel, "height", axis=1, tiled=True)
+    nodes = lax.axis_size("height")
+    cards = [(to_i, (to_i + 1) % nodes) for to_i in range(nodes)]
+    pool = [(to_i, (to_i - 1) % nodes) for to_i in range(nodes)]
+    main, arr_next = ([kernel], [kernel])
+    for _ in range(nodes // 2):
+        main.append(lax.ppermute(main[-1], "height", cards))
+    p = 0
+    while p < (nodes - 1) // 2:
+        arr_next.append(lax.ppermute(arr_next[-1], "height", pool))
+        p += 1
+    gathered = jnp.roll(
+        jnp.concatenate([*main[::-1], *arr_next[1:]], axis=1),
+        shift=(lax.axis_index("height") - nodes // 2) * kernel.shape[1],
+        axis=1,
+    )
     return tap_sum(padded, gathered, out_rows)
 
 

time: 293 us -> 457 us (1.56)
  starting transfers between devices: 5.41 us -> 197 us
  waiting for transfers between devices: 121 us -> 56 us
  other arithmetic: 1.75 us -> 35.6 us
  matrix products: 77.5 us -> 54.1 us
  local copies, waits for them, and re-layouts: 5.75 us -> 28.8 us
  blocking collectives: 67.8 us -> 82.7 us
  between operations: 13.7 us -> 0.96 us
    ppermute x0 -> x30, starting transfers between devices: none -> 191 us  [the longest x16 126 us: convolve(): main.append(lax.ppermute(main[-1], 'height', cards))]
    all_gather x2 -> x0, waiting for transfers between devices: 117 us -> none  [convolve(): gathered = lax.all_gather(kernel, 'height', axis=1, tiled=True)]
    ppermute x2, waiting for transfers between devices: 2.1 us -> 36.4 us  [with_halo(): lax.ppermute(head, axis, [((i + 1) % count, i) for i in range(ends)])]
    concatenate x0 -> x2, other arithmetic: none -> 31.7 us  [convolve(): jnp.roll(jnp.concatenate([*main[::-1], *arr_next[1:]], axis=1), shift=(la...]
    dot_general x54, matrix products: 77.5 us -> 54.1 us  [tap_sum(): jnp.einsum('fhwk,ko->fhwo', window, kernel_part[9 * step_t + 3 * step_h +...]
    unnamed x20 -> x112, local copies, waits for them, and re-layouts: 0.04 us -> 22.8 us
    ppermute x0 -> x30, waiting for transfers between devices: none -> 18.5 us  [the longest x16 18.4 us: convolve(): main.append(lax.ppermute(main[-1], 'height', cards))]
    psum x2, blocking collectives: 67.8 us -> 82.7 us  [moments(): summed, spread = lax.psum((chan_sums, squares), 'height')]
  transfers between devices with their start and end apart: 6 -> 34, of which waited for: 3 -> 4; matrix products, arithmetic and copies ran while one was open for 15% -> 18% of each run, Pallas kernels for 0% -> 0%
where the time goes in v1:
time: 457 us; the launch traced here: 455 us
  starting transfers between devices  197 us (43%)
  blocking collectives  82.7 us (18%)
  waiting for transfers between devices  56 us (12%)
  matrix products  54.1 us (12%)
  other arithmetic  35.6 us (8%)
  local copies, waits for them, and re-layouts  28.8 us (6%)
    ppermute x16, starting transfers between devices, convolve(): main.append(lax.ppermute(main[-1], 'height', cards))  126 us
    psum x2, blocking collectives, moments(): summed, spread = lax.psum((chan_sums, squares), 'height')  82.7 us
    ppermute x14, starting transfers between devices, convolve(): arr_next.append(lax.ppermute(arr_next[-1], 'height', pool))  65.3 us
    dot_general x54, matrix products, tap_sum(): jnp.einsum('fhwk,ko->fhwo', window, kernel_part[9 * step_t + 3 * step_h +...  54.1 us
    ppermute x2, waiting for transfers between devices, with_halo(): lax.ppermute(head, axis, [((i + 1) % count, i) for i in range(ends)])  36.4 us
    concatenate x2, other arithmetic, convolve(): jnp.roll(jnp.concatenate([*main[::-1], *arr_next[1:]], axis=1), shift=(la...  31.7 us
    unnamed x112, local copies, waits for them, and re-layouts  22.8 us
    ppermute x16, waiting for transfers between devices, convolve(): main.append(lax.ppermute(main[-1], 'height', cards))  18.4 us
  transfers between devices with their start and end apart: 34, of which 4 were waited for; matrix products, arithmetic and copies ran while one was open for 18% of the time, Pallas kernels for 0%

profile of v1, /device:TPU:0, one launch (start us, length us, event | category | flops | bytes accessed | tf_op | source)
XLA Modules:
  0.0 455.4 jit_solution(3857639946892390162)
XLA Ops:
  0.5 2.6 collective-permute-start.19
  3.1 13.3 %collective-permute-done.2 = bf16[27,32,512]{2,1,0:T(8,128)(2,1)S(1)} collective-permute-done((bf16[27,32,512]{2,1,0:T(8,128)(2,1)}, bf16[27,32,512]{2,1,0:T(8,128)(2,1)S(1)}, u32[]{:S(2)}, u32[]{:S(2)}) %collective-permute-start.2) | collective-permute-done | bytes 884768 | tf_op jit(solution)/shard_map/ppermute | solution.py:78
  16.4 4.4 collective-permute-start.10
  20.9 5.1 %collective-permute-done.19 = bf16[27,32,512]{2,1,0:T(8,128)(2,1)S(1)} collective-permute-done((bf16[27,32,512]{2,1,0:T(8,128)(2,1)}, bf16[27,32,512]{2,1,0:T(8,128)(2,1)S(1)}, u32[]{:S(2)}, u32[]{:S(2)}) %collective-permute-start.19) | collective-permute-done | bytes 884768 | tf_op jit(solution)/shard_map/ppermute | solution.py:78
  26.9 15.9 %collective-permute-start.20 = (bf16[27,32,512]{2,1,0:T(8,128)(2,1)S(1)}, bf16[27,32,512]{2,1,0:T(8,128)(2,1)S(1)}, u32[]{:S(2)}, u32[]{:S(2)}) collective-permute-start(bf16[27,32,512]{2,1,0:T(8,128)(2,1)S(1)} %collective-permute-done.19), channel_id=1, source_target_pairs={{0,1},{1,2},{2,3},{3,4},{4,5},{5,6},{6,7},{7,8},{8,9},{9,10},{10,1... | collective-permute-start | bytes 2654216 | tf_op jit(solution)/shard_map/ppermute | solution.py:78
  42.7 8.5 %collective-permute-start.4 = (bf16[27,32,512]{2,1,0:T(8,128)(2,1)S(1)}, bf16[27,32,512]{2,1,0:T(8,128)(2,1)S(1)}, u32[]{:S(2)}, u32[]{:S(2)}) collective-permute-start(bf16[27,32,512]{2,1,0:T(8,128)(2,1)S(1)} %collective-permute-done.3), channel_id=1, source_target_pairs={{0,1},{1,2},{2,3},{3,4},{4,5},{5,6},{6,7},{7,8},{8,9},{9,10},{10,1... | collective-permute-start | bytes 2654216 | tf_op jit(solution)/shard_map/ppermute | solution.py:78
  51.2 14.0 %collective-permute-start.28 = (bf16[27,32,512]{2,1,0:T(8,128)(2,1)S(1)}, bf16[27,32,512]{2,1,0:T(8,128)(2,1)S(1)}, u32[]{:S(2)}, u32[]{:S(2)}) collective-permute-start(bf16[27,32,512]{2,1,0:T(8,128)(2,1)S(1)} %collective-permute-done.27), channel_id=1, source_target_pairs={{0,15},{1,0},{2,1},{3,2},{4,3},{5,4},{6,5},{7,6},{8,7},{9,8},{10,9... | collective-permute-start | bytes 2654216 | tf_op jit(solution)/shard_map/ppermute | solution.py:81
  65.3 14.3 %collective-permute-start.21 = (bf16[27,32,512]{2,1,0:T(8,128)(2,1)S(1)}, bf16[27,32,512]{2,1,0:T(8,128)(2,1)S(1)}, u32[]{:S(2)}, u32[]{:S(2)}) collective-permute-start(bf16[27,32,512]{2,1,0:T(8,128)(2,1)S(1)} %collective-permute-done.20), channel_id=1, source_target_pairs={{0,1},{1,2},{2,3},{3,4},{4,5},{5,6},{6,7},{7,8},{8,9},{9,10},{10,1... | collective-permute-start | bytes 2654216 | tf_op jit(solution)/shard_map/ppermute | solution.py:78
  79.7 9.5 %collective-permute-start.5 = (bf16[27,32,512]{2,1,0:T(8,128)(2,1)S(1)}, bf16[27,32,512]{2,1,0:T(8,128)(2,1)S(1)}, u32[]{:S(2)}, u32[]{:S(2)}) collective-permute-start(bf16[27,32,512]{2,1,0:T(8,128)(2,1)S(1)} %collective-permute-done.4), channel_id=1, source_target_pairs={{0,1},{1,2},{2,3},{3,4},{4,5},{5,6},{6,7},{7,8},{8,9},{9,10},{10,1... | collective-permute-start | bytes 2654216 | tf_op jit(solution)/shard_map/ppermute | solution.py:78
  89.2 13.9 %collective-permute-start.29 = (bf16[27,32,512]{2,1,0:T(8,128)(2,1)S(1)}, bf16[27,32,512]{2,1,0:T(8,128)(2,1)S(1)}, u32[]{:S(2)}, u32[]{:S(2)}) collective-permute-start(bf16[27,32,512]{2,1,0:T(8,128)(2,1)S(1)} %collective-permute-done.28), channel_id=1, source_target_pairs={{0,15},{1,0},{2,1},{3,2},{4,3},{5,4},{6,5},{7,6},{8,7},{9,8},{10,9... | collective-permute-start | bytes 2654216 | tf_op jit(solution)/shard_map/ppermute | solution.py:81
  103.1 14.5 %collective-permute-start.22 = (bf16[27,32,512]{2,1,0:T(8,128)(2,1)S(1)}, bf16[27,32,512]{2,1,0:T(8,128)(2,1)S(1)}, u32[]{:S(2)}, u32[]{:S(2)}) collective-permute-start(bf16[27,32,512]{2,1,0:T(8,128)(2,1)S(1)} %collective-permute-done.21), channel_id=1, source_target_pairs={{0,1},{1,2},{2,3},{3,4},{4,5},{5,6},{6,7},{7,8},{8,9},{9,10},{10,1... | collective-permute-start | bytes 2654216 | tf_op jit(solution)/shard_map/ppermute | solution.py:78
  117.6 9.5 %collective-permute-start.6 = (bf16[27,32,512]{2,1,0:T(8,128)(2,1)S(1)}, bf16[27,32,512]{2,1,0:T(8,128)(2,1)S(1)}, u32[]{:S(2)}, u32[]{:S(2)}) collective-permute-start(bf16[27,32,512]{2,1,0:T(8,128)(2,1)S(1)} %collective-permute-done.5), channel_id=1, source_target_pairs={{0,1},{1,2},{2,3},{3,4},{4,5},{5,6},{6,7},{7,8},{8,9},{9,10},{10,1... | collective-permute-start | bytes 2654216 | tf_op jit(solution)/shard_map/ppermute | solution.py:78
  127.1 13.9 %collective-permute-start.30 = (bf16[27,32,512]{2,1,0:T(8,128)(2,1)S(1)}, bf16[27,32,512]{2,1,0:T(8,128)(2,1)S(1)}, u32[]{:S(2)}, u32[]{:S(2)}) collective-permute-start(bf16[27,32,512]{2,1,0:T(8,128)(2,1)S(1)} %collective-permute-done.29), channel_id=1, source_target_pairs={{0,15},{1,0},{2,1},{3,2},{4,3},{5,4},{6,5},{7,6},{8,7},{9,8},{10,9... | collective-permute-start | bytes 2654216 | tf_op jit(solution)/shard_map/ppermute | solution.py:81
  141.0 14.5 %collective-permute-start.23 = (bf16[27,32,512]{2,1,0:T(8,128)(2,1)S(1)}, bf16[27,32,512]{2,1,0:T(8,128)(2,1)}, u32[]{:S(2)}, u32[]{:S(2)}) collective-permute-start(bf16[27,32,512]{2,1,0:T(8,128)(2,1)S(1)} %collective-permute-done.22), channel_id=1, source_target_pairs={{0,1},{1,2},{2,3},{3,4},{4,5},{5,6},{6,7},{7,8},{8,9},{9,10},{10,1... | collective-permute-start | bytes 2654216 | tf_op jit(solution)/shard_map/ppermute | solution.py:78
  155.5 9.5 %collective-permute-start.7 = (bf16[27,32,512]{2,1,0:T(8,128)(2,1)S(1)}, bf16[27,32,512]{2,1,0:T(8,128)(2,1)}, u32[]{:S(2)}, u32[]{:S(2)}) collective-permute-start(bf16[27,32,512]{2,1,0:T(8,128)(2,1)S(1)} %collective-permute-done.6), channel_id=1, source_target_pairs={{0,1},{1,2},{2,3},{3,4},{4,5},{5,6},{6,7},{7,8},{8,9},{9,10},{10,1... | collective-permute-start | bytes 2654216 | tf_op jit(solution)/shard_map/ppermute | solution.py:78
  165.0 13.9 %collective-permute-start.31 = (bf16[27,32,512]{2,1,0:T(8,128)(2,1)S(1)}, bf16[27,32,512]{2,1,0:T(8,128)(2,1)S(1)}, u32[]{:S(2)}, u32[]{:S(2)}) collective-permute-start(bf16[27,32,512]{2,1,0:T(8,128)(2,1)S(1)} %collective-permute-done.30), channel_id=1, source_target_pairs={{0,15},{1,0},{2,1},{3,2},{4,3},{5,4},{6,5},{7,6},{8,7},{9,8},{10,9... | collective-permute-start | bytes 2654216 | tf_op jit(solution)/shard_map/ppermute | solution.py:81
  178.9 14.5 %collective-permute-start.24 = (bf16[27,32,512]{2,1,0:T(8,128)(2,1)}, bf16[27,32,512]{2,1,0:T(8,128)(2,1)}, u32[]{:S(2)}, u32[]{:S(2)}) collective-permute-start(bf16[27,32,512]{2,1,0:T(8,128)(2,1)} %collective-permute-done.23), channel_id=1, source_target_pairs={{0,1},{1,2},{2,3},{3,4},{4,5},{5,6},{6,7},{7,8},{8,9},{9,10},{10,1... | collective-permute-start | bytes 2654216 | tf_op jit(solution)/shard_map/ppermute | solution.py:78
  193.4 9.5 %collective-permute-start.8 = (bf16[27,32,512]{2,1,0:T(8,128)(2,1)}, bf16[27,32,512]{2,1,0:T(8,128)(2,1)}, u32[]{:S(2)}, u32[]{:S(2)}) collective-permute-start(bf16[27,32,512]{2,1,0:T(8,128)(2,1)} %collective-permute-done.7), channel_id=1, source_target_pairs={{0,1},{1,2},{2,3},{3,4},{4,5},{5,6},{6,7},{7,8},{8,9},{9,10},{10,1... | collective-permute-start | bytes 2654216 | tf_op jit(solution)/shard_map/ppermute | solution.py:78
  204.5 42.2 %all-reduce.3 = (f32[32]{0:T(128)S(1)}, f32[32]{0:T(128)S(1)}) all-reduce(f32[32]{0:T(128)S(1)} %reduce_sum.75, f32[32]{0:T(128)S(1)} %reduce_sum.73), channel_id=1, replica_groups=mesh['groups'=2,'height'=16] {'height'}, use_global_device_ids=true, to_apply=%region_5.0 | all-reduce | flops 64 | bytes 512 | tf_op jit(solution)/shard_map/psum | solution.py:32
  249.1 1.7 collective-permute-start.9
  250.8 2.0 collective-permute-start
  255.2 36.4 %collective-permute-done.1 = bf16[3,1,80,512]{3,2,1,0:T(8,128)(2,1)S(1)} collective-permute-done((bf16[3,1,80,512]{3,2,1,0:T(8,128)(2,1)S(1)}, bf16[3,1,80,512]{3,2,1,0:T(8,128)(2,1)S(1)}, u32[]{:S(2)}, u32[]{:S(2)}) %collective-permute-start.1) | collective-permute-done | bytes 245792 | tf_op jit(solution)/shard_map/ppermute | solution.py:19
  291.9 2.2 collective-permute-start.16
  294.1 2.6 collective-permute-start.33
  308.6 15.8 %fusion.1 = bf16[27,512,512]{2,1,0:T(8,128)(2,1)S(1)} fusion(s32[]{:T(128)S(6)} %select_n.13, bf16[27,512,512]{2,1,0:T(8,128)(2,1)S(1)} %constant_dynamic-update-slice_fusion), kind=kLoop, calls=%fused_computation.5 | loop fusion | flops 28311552 | bytes 28311556 | tf_op jit(solution)/shard_map/jit(_roll_dynamic)/concatenate | solution.py:83
  335.1 1.5 fusion.92
  344.4 5.5 %convolution_add_fusion.3 = f32[3,2,80,512]{3,2,1,0:T(8,128)S(1)} fusion(bf16[3,2,80,512]{3,2,1,0:T(8,128)(2,1)S(1)} %fusion.30, f32[3,2,80,512]{3,2,1,0:T(8,128)S(1)} %fusion.73, f32[3,2,80,512]{3,2,1,0:T(8,128)S(1)} %fusion.74, f32[3,2,80,512]{3,2,1,0:T(8,128)} %fusion.32, f32[3,2,80,512]{3,2,1,0:T(8,128)S(1)} %fusion.75, ...), kind=kOutput, calls=%fused_computation.26 | convolution fusion | flops 257064960 | bytes 23625728 | tf_op jit(solution)/shard_map/fhwk,ko->fhwo/dot_general | solution.py:63
  351.6 40.5 %all-reduce.2 = (f32[32]{0:T(128)S(1)}, f32[32]{0:T(128)S(1)}) all-reduce(f32[32]{0:T(128)S(1)} %reduce_sum.79, f32[32]{0:T(128)S(1)} %reduce_sum.77), channel_id=1, replica_groups=mesh['groups'=2,'height'=16] {'height'}, use_global_device_ids=true, to_apply=%region_11.13 | all-reduce | flops 64 | bytes 512 | tf_op jit(solution)/shard_map/psum | solution.py:32
  407.2 16.0 %fusion = bf16[27,512,512]{2,1,0:T(8,128)(2,1)S(1)} fusion(s32[]{:T(128)S(6)} %select_n.13, bf16[27,512,512]{2,1,0:T(8,128)(2,1)S(1)} %constant_dynamic-update-slice_fusion.16), kind=kLoop, calls=%fused_computation.4 | loop fusion | flops 28311552 | bytes 28311556 | tf_op jit(solution)/shard_map/jit(_roll_dynamic)/concatenate | solution.py:83
  428.1 1.5 fusion.58
  444.3 5.7 %convolution_add_fusion.1 = f32[3,2,80,512]{3,2,1,0:T(8,128)S(1)} fusion(bf16[3,2,80,512]{3,2,1,0:T(8,128)(2,1)S(1)} %fusion.20, f32[3,2,80,512]{3,2,1,0:T(8,128)} %fusion.50, f32[3,2,80,512]{3,2,1,0:T(8,128)} %fusion.51, f32[3,2,80,512]{3,2,1,0:T(8,128)} %fusion.40, f32[3,2,80,512]{3,2,1,0:T(8,128)} %fusion.52, f32[3,2,80,512]{3,2,1,0:T(8,128)} %fusion.53, ...), kind=kOutput, calls=%fused_computation.20 | convolution fusion | flops 257064960 | bytes 23625728 | tf_op jit(solution)/shard_map/fhwk,ko->fhwo/dot_general | solution.py:63
  453.2 2.2 reshape.33
  (238 shorter events, 77.5 us)
Async XLA Ops:
  0.5 25.5 %collective-permute-start.19 = (bf16[27,32,512]{2,1,0:T(8,128)(2,1)}, bf16[27,32,512]{2,1,0:T(8,128)(2,1)S(1)}, u32[]{:S(2)}, u32[]{:S(2)}) collective-permute-start(bf16[27,32,512]{2,1,0:T(8,128)(2,1)} %param.18), channel_id=1, source_target_pairs={{0,1},{1,2},{2,3},{3,4},{4,5},{5,6},{6,7},{7,8},{8,9},{9,10},{10,1... | collective-permute-start | bytes 2654216 | tf_op jit(solution)/shard_map/ppermute | solution.py:78
  16.4 26.4 %collective-permute-start.3 = (bf16[27,32,512]{2,1,0:T(8,128)(2,1)S(1)}, bf16[27,32,512]{2,1,0:T(8,128)(2,1)S(1)}, u32[]{:S(2)}, u32[]{:S(2)}) collective-permute-start(bf16[27,32,512]{2,1,0:T(8,128)(2,1)S(1)} %collective-permute-done.2), channel_id=1, source_target_pairs={{0,1},{1,2},{2,3},{3,4},{4,5},{5,6},{6,7},{7,8},{8,9},{9,10},{10,1... | collective-permute-start | bytes 2654216 | tf_op jit(solution)/shard_map/ppermute | solution.py:78
  16.4 34.8 %collective-permute-start.10 = (bf16[27,32,512]{2,1,0:T(8,128)(2,1)}, bf16[27,32,512]{2,1,0:T(8,128)(2,1)S(1)}, u32[]{:S(2)}, u32[]{:S(2)}) collective-permute-start(bf16[27,32,512]{2,1,0:T(8,128)(2,1)} %param.14), channel_id=1, source_target_pairs={{0,15},{1,0},{2,1},{3,2},{4,3},{5,4},{6,5},{7,6},{8,7},{9,8},{10,9... | collective-permute-start | bytes 2654216 | tf_op jit(solution)/shard_map/ppermute | solution.py:81
  20.8 30.4 %collective-permute-start.27 = (bf16[27,32,512]{2,1,0:T(8,128)(2,1)}, bf16[27,32,512]{2,1,0:T(8,128)(2,1)S(1)}, u32[]{:S(2)}, u32[]{:S(2)}) collective-permute-start(bf16[27,32,512]{2,1,0:T(8,128)(2,1)} %param.18), channel_id=1, source_target_pairs={{0,15},{1,0},{2,1},{3,2},{4,3},{5,4},{6,5},{7,6},{8,7},{9,8},{10,9... | collective-permute-start | bytes 2654216 | tf_op jit(solution)/shard_map/ppermute | solution.py:81
  26.9 38.4 %collective-permute-start.20 = (bf16[27,32,512]{2,1,0:T(8,128)(2,1)S(1)}, bf16[27,32,512]{2,1,0:T(8,128)(2,1)S(1)}, u32[]{:S(2)}, u32[]{:S(2)}) collective-permute-start(bf16[27,32,512]{2,1,0:T(8,128)(2,1)S(1)} %collective-permute-done.19), channel_id=1, source_target_pairs={{0,1},{1,2},{2,3},{3,4},{4,5},{5,6},{6,7},{7,8},{8,9},{9,10},{10,1... | collective-permute-start | bytes 2654216 | tf_op jit(solution)/shard_map/ppermute | solution.py:78
  42.7 36.9 %collective-permute-start.4 = (bf16[27,32,512]{2,1,0:T(8,128)(2,1)S(1)}, bf16[27,32,512]{2,1,0:T(8,128)(2,1)S(1)}, u32[]{:S(2)}, u32[]{:S(2)}) collective-permute-start(bf16[27,32,512]{2,1,0:T(8,128)(2,1)S(1)} %collective-permute-done.3), channel_id=1, source_target_pairs={{0,1},{1,2},{2,3},{3,4},{4,5},{5,6},{6,7},{7,8},{8,9},{9,10},{10,1... | collective-permute-start | bytes 2654216 | tf_op jit(solution)/shard_map/ppermute | solution.py:78
  51.2 37.9 %collective-permute-start.11 = (bf16[27,32,512]{2,1,0:T(8,128)(2,1)S(1)}, bf16[27,32,512]{2,1,0:T(8,128)(2,1)S(1)}, u32[]{:S(2)}, u32[]{:S(2)}) collective-permute-start(bf16[27,32,512]{2,1,0:T(8,128)(2,1)S(1)} %collective-permute-done.10), channel_id=1, source_target_pairs={{0,15},{1,0},{2,1},{3,2},{4,3},{5,4},{6,5},{7,6},{8,7},{9,8},{10,9... | collective-permute-start | bytes 2654216 | tf_op jit(solution)/shard_map/ppermute | solution.py:81
  51.2 37.9 %collective-permute-start.28 = (bf16[27,32,512]{2,1,0:T(8,128)(2,1)S(1)}, bf16[27,32,512]{2,1,0:T(8,128)(2,1)S(1)}, u32[]{:S(2)}, u32[]{:S(2)}) collective-permute-start(bf16[27,32,512]{2,1,0:T(8,128)(2,1)S(1)} %collective-permute-done.27), channel_id=1, source_target_pairs={{0,15},{1,0},{2,1},{3,2},{4,3},{5,4},{6,5},{7,6},{8,7},{9,8},{10,9... | collective-permute-start | bytes 2654216 | tf_op jit(solution)/shard_map/ppermute | solution.py:81
  65.3 37.8 %collective-permute-start.21 = (bf16[27,32,512]{2,1,0:T(8,128)(2,1)S(1)}, bf16[27,32,512]{2,1,0:T(8,128)(2,1)S(1)}, u32[]{:S(2)}, u32[]{:S(2)}) collective-permute-start(bf16[27,32,512]{2,1,0:T(8,128)(2,1)S(1)} %collective-permute-done.20), channel_id=1, source_target_pairs={{0,1},{1,2},{2,3},{3,4},{4,5},{5,6},{6,7},{7,8},{8,9},{9,10},{10,1... | collective-permute-start | bytes 2654216 | tf_op jit(solution)/shard_map/ppermute | solution.py:78
  79.7 37.9 %collective-permute-start.5 = (bf16[27,32,512]{2,1,0:T(8,128)(2,1)S(1)}, bf16[27,32,512]{2,1,0:T(8,128)(2,1)S(1)}, u32[]{:S(2)}, u32[]{:S(2)}) collective-permute-start(bf16[27,32,512]{2,1,0:T(8,128)(2,1)S(1)} %collective-permute-done.4), channel_id=1, source_target_pairs={{0,1},{1,2},{2,3},{3,4},{4,5},{5,6},{6,7},{7,8},{8,9},{9,10},{10,1... | collective-permute-start | bytes 2654216 | tf_op jit(solution)/shard_map/ppermute | solution.py:78
  89.1 37.9 %collective-permute-start.12 = (bf16[27,32,512]{2,1,0:T(8,128)(2,1)S(1)}, bf16[27,32,512]{2,1,0:T(8,128)(2,1)S(1)}, u32[]{:S(2)}, u32[]{:S(2)}) collective-permute-start(bf16[27,32,512]{2,1,0:T(8,128)(2,1)S(1)} %collective-permute-done.11), channel_id=1, source_target_pairs={{0,15},{1,0},{2,1},{3,2},{4,3},{5,4},{6,5},{7,6},{8,7},{9,8},{10,9... | collective-permute-start | bytes 2654216 | tf_op jit(solution)/shard_map/ppermute | solution.py:81
  89.2 37.9 %collective-permute-start.29 = (bf16[27,32,512]{2,1,0:T(8,128)(2,1)S(1)}, bf16[27,32,512]{2,1,0:T(8,128)(2,1)S(1)}, u32[]{:S(2)}, u32[]{:S(2)}) collective-permute-start(bf16[27,32,512]{2,1,0:T(8,128)(2,1)S(1)} %collective-permute-done.28), channel_id=1, source_target_pairs={{0,15},{1,0},{2,1},{3,2},{4,3},{5,4},{6,5},{7,6},{8,7},{9,8},{10,9... | collective-permute-start | bytes 2654216 | tf_op jit(solution)/shard_map/ppermute | solution.py:81
  103.1 37.9 %collective-permute-start.22 = (bf16[27,32,512]{2,1,0:T(8,128)(2,1)S(1)}, bf16[27,32,512]{2,1,0:T(8,128)(2,1)S(1)}, u32[]{:S(2)}, u32[]{:S(2)}) collective-permute-start(bf16[27,32,512]{2,1,0:T(8,128)(2,1)S(1)} %collective-permute-done.21), channel_id=1, source_target_pairs={{0,1},{1,2},{2,3},{3,4},{4,5},{5,6},{6,7},{7,8},{8,9},{9,10},{10,1... | collective-permute-start | bytes 2654216 | tf_op jit(solution)/shard_map/ppermute | solution.py:78
  117.6 37.9 %collective-permute-start.6 = (bf16[27,32,512]{2,1,0:T(8,128)(2,1)S(1)}, bf16[27,32,512]{2,1,0:T(8,128)(2,1)S(1)}, u32[]{:S(2)}, u32[]{:S(2)}) collective-permute-start(bf16[27,32,512]{2,1,0:T(8,128)(2,1)S(1)} %collective-permute-done.5), channel_id=1, source_target_pairs={{0,1},{1,2},{2,3},{3,4},{4,5},{5,6},{6,7},{7,8},{8,9},{9,10},{10,1... | collective-permute-start | bytes 2654216 | tf_op jit(solution)/shard_map/ppermute | solution.py:78
  127.0 37.9 %collective-permute-start.13 = (bf16[27,32,512]{2,1,0:T(8,128)(2,1)S(1)}, bf16[27,32,512]{2,1,0:T(8,128)(2,1)}, u32[]{:S(2)}, u32[]{:S(2)}) collective-permute-start(bf16[27,32,512]{2,1,0:T(8,128)(2,1)S(1)} %collective-permute-done.12), channel_id=1, source_target_pairs={{0,15},{1,0},{2,1},{3,2},{4,3},{5,4},{6,5},{7,6},{8,7},{9,8},{10,9... | collective-permute-start | bytes 2654216 | tf_op jit(solution)/shard_map/ppermute | solution.py:81
  127.1 37.9 %collective-permute-start.30 = (bf16[27,32,512]{2,1,0:T(8,128)(2,1)S(1)}, bf16[27,32,512]{2,1,0:T(8,128)(2,1)S(1)}, u32[]{:S(2)}, u32[]{:S(2)}) collective-permute-start(bf16[27,32,512]{2,1,0:T(8,128)(2,1)S(1)} %collective-permute-done.29), channel_id=1, source_target_pairs={{0,15},{1,0},{2,1},{3,2},{4,3},{5,4},{6,5},{7,6},{8,7},{9,8},{10,9... | collective-permute-start | bytes 2654216 | tf_op jit(solution)/shard_map/ppermute | solution.py:81
  141.0 37.9 %collective-permute-start.23 = (bf16[27,32,512]{2,1,0:T(8,128)(2,1)S(1)}, bf16[27,32,512]{2,1,0:T(8,128)(2,1)}, u32[]{:S(2)}, u32[]{:S(2)}) collective-permute-start(bf16[27,32,512]{2,1,0:T(8,128)(2,1)S(1)} %collective-permute-done.22), channel_id=1, source_target_pairs={{0,1},{1,2},{2,3},{3,4},{4,5},{5,6},{6,7},{7,8},{8,9},{9,10},{10,1... | collective-permute-start | bytes 2654216 | tf_op jit(solution)/shard_map/ppermute | solution.py:78
  155.5 37.9 %collective-permute-start.7 = (bf16[27,32,512]{2,1,0:T(8,128)(2,1)S(1)}, bf16[27,32,512]{2,1,0:T(8,128)(2,1)}, u32[]{:S(2)}, u32[]{:S(2)}) collective-permute-start(bf16[27,32,512]{2,1,0:T(8,128)(2,1)S(1)} %collective-permute-done.6), channel_id=1, source_target_pairs={{0,1},{1,2},{2,3},{3,4},{4,5},{5,6},{6,7},{7,8},{8,9},{9,10},{10,1... | collective-permute-start | bytes 2654216 | tf_op jit(solution)/shard_map/ppermute | solution.py:78
  165.0 83.5 %collective-permute-start.14 = (bf16[27,32,512]{2,1,0:T(8,128)(2,1)}, bf16[27,32,512]{2,1,0:T(8,128)(2,1)}, u32[]{:S(2)}, u32[]{:S(2)}) collective-permute-start(bf16[27,32,512]{2,1,0:T(8,128)(2,1)} %collective-permute-done.13), channel_id=1, source_target_pairs={{0,15},{1,0},{2,1},{3,2},{4,3},{5,4},{6,5},{7,6},{8,7},{9,8},{10,9... | collective-permute-start | bytes 2654216 | tf_op jit(solution)/shard_map/ppermute | solution.py:81
  165.0 83.5 %collective-permute-start.31 = (bf16[27,32,512]{2,1,0:T(8,128)(2,1)S(1)}, bf16[27,32,512]{2,1,0:T(8,128)(2,1)S(1)}, u32[]{:S(2)}, u32[]{:S(2)}) collective-permute-start(bf16[27,32,512]{2,1,0:T(8,128)(2,1)S(1)} %collective-permute-done.30), channel_id=1, source_target_pairs={{0,15},{1,0},{2,1},{3,2},{4,3},{5,4},{6,5},{7,6},{8,7},{9,8},{10,9... | collective-permute-start | bytes 2654216 | tf_op jit(solution)/shard_map/ppermute | solution.py:81
  178.9 69.7 %collective-permute-start.24 = (bf16[27,32,512]{2,1,0:T(8,128)(2,1)}, bf16[27,32,512]{2,1,0:T(8,128)(2,1)}, u32[]{:S(2)}, u32[]{:S(2)}) collective-permute-start(bf16[27,32,512]{2,1,0:T(8,128)(2,1)} %collective-permute-done.23), channel_id=1, source_target_pairs={{0,1},{1,2},{2,3},{3,4},{4,5},{5,6},{6,7},{7,8},{8,9},{9,10},{10,1... | collective-permute-start | bytes 2654216 | tf_op jit(solution)/shard_map/ppermute | solution.py:78
  193.4 55.7 %collective-permute-start.8 = (bf16[27,32,512]{2,1,0:T(8,128)(2,1)}, bf16[27,32,512]{2,1,0:T(8,128)(2,1)}, u32[]{:S(2)}, u32[]{:S(2)}) collective-permute-start(bf16[27,32,512]{2,1,0:T(8,128)(2,1)} %collective-permute-done.7), channel_id=1, source_target_pairs={{0,1},{1,2},{2,3},{3,4},{4,5},{5,6},{6,7},{7,8},{8,9},{9,10},{10,1... | collective-permute-start | bytes 2654216 | tf_op jit(solution)/shard_map/ppermute | solution.py:78
  248.4 43.5 %collective-permute-start.15 = (bf16[27,32,512]{2,1,0:T(8,128)(2,1)}, bf16[27,32,512]{2,1,0:T(8,128)(2,1)}, u32[]{:S(2)}, u32[]{:S(2)}) collective-permute-start(bf16[27,32,512]{2,1,0:T(8,128)(2,1)} %collective-permute-done.14), channel_id=1, source_target_pairs={{0,15},{1,0},{2,1},{3,2},{4,3},{5,4},{6,5},{7,6},{8,7},{9,8},{10,9... | collective-permute-start | bytes 2654216 | tf_op jit(solution)/shard_map/ppermute | solution.py:81
  248.5 45.6 %collective-permute-start.32 = (bf16[27,32,512]{2,1,0:T(8,128)(2,1)S(1)}, bf16[27,32,512]{2,1,0:T(8,128)(2,1)}, u32[]{:S(2)}, u32[]{:S(2)}) collective-permute-start(bf16[27,32,512]{2,1,0:T(8,128)(2,1)S(1)} %collective-permute-done.31), channel_id=1, source_target_pairs={{0,15},{1,0},{2,1},{3,2},{4,3},{5,4},{6,5},{7,6},{8,7},{9,8},{10,9... | collective-permute-start | bytes 2654216 | tf_op jit(solution)/shard_map/ppermute | solution.py:81
  248.6 48.1 %collective-permute-start.25 = (bf16[27,32,512]{2,1,0:T(8,128)(2,1)}, bf16[27,32,512]{2,1,0:T(8,128)(2,1)}, u32[]{:S(2)}, u32[]{:S(2)}) collective-permute-start(bf16[27,32,512]{2,1,0:T(8,128)(2,1)} %collective-permute-done.24), channel_id=1, source_target_pairs={{0,1},{1,2},{2,3},{3,4},{4,5},{5,6},{6,7},{7,8},{8,9},{9,10},{10,1... | collective-permute-start | bytes 2654216 | tf_op jit(solution)/shard_map/ppermute | solution.py:78
  249.1 48.5 %collective-permute-start.9 = (bf16[27,32,512]{2,1,0:T(8,128)(2,1)}, bf16[27,32,512]{2,1,0:T(8,128)(2,1)}, u32[]{:S(2)}, u32[]{:S(2)}) collective-permute-start(bf16[27,32,512]{2,1,0:T(8,128)(2,1)} %collective-permute-done.8), channel_id=1, source_target_pairs={{0,1},{1,2},{2,3},{3,4},{4,5},{5,6},{6,7},{7,8},{8,9},{9,10},{10,1... | collective-permute-start | bytes 2654216 | tf_op jit(solution)/shard_map/ppermute | solution.py:78
  253.9 37.8 %collective-permute-start.1 = (bf16[3,1,80,512]{3,2,1,0:T(8,128)(2,1)S(1)}, bf16[3,1,80,512]{3,2,1,0:T(8,128)(2,1)S(1)}, u32[]{:S(2)}, u32[]{:S(2)}) collective-permute-start(bf16[3,1,80,512]{3,2,1,0:T(8,128)(2,1)S(1)} %get-tuple-element.17), channel_id=1, source_target_pairs={{1,0},{2,1},{3,2},{4,3},{5,4},{6,5},{7,6},{8,7},{9,8},{10,9},{11,1... | collective-permute-start | bytes 737288 | tf_op jit(solution)/shard_map/ppermute | solution.py:19
  291.9 16.6 %collective-permute-start.16 = (bf16[27,32,512]{2,1,0:T(8,128)(2,1)}, bf16[27,32,512]{2,1,0:T(8,128)(2,1)S(1)}, u32[]{:S(2)}, u32[]{:S(2)}) collective-permute-start(bf16[27,32,512]{2,1,0:T(8,128)(2,1)} %collective-permute-done.15), channel_id=1, source_target_pairs={{0,15},{1,0},{2,1},{3,2},{4,3},{5,4},{6,5},{7,6},{8,7},{9,8},{10,9... | collective-permute-start | bytes 2654216 | tf_op jit(solution)/shard_map/ppermute | solution.py:81
  294.1 111.7 %collective-permute-start.33 = (bf16[27,32,512]{2,1,0:T(8,128)(2,1)}, bf16[27,32,512]{2,1,0:T(8,128)(2,1)}, u32[]{:S(2)}, u32[]{:S(2)}) collective-permute-start(bf16[27,32,512]{2,1,0:T(8,128)(2,1)} %collective-permute-done.32), channel_id=1, source_target_pairs={{0,15},{1,0},{2,1},{3,2},{4,3},{5,4},{6,5},{7,6},{8,7},{9,8},{10,9... | collective-permute-start | bytes 2654216 | tf_op jit(solution)/shard_map/ppermute | solution.py:81
  296.7 98.7 %collective-permute-start.26 = (bf16[27,32,512]{2,1,0:T(8,128)(2,1)}, bf16[27,32,512]{2,1,0:T(8,128)(2,1)}, u32[]{:S(2)}, u32[]{:S(2)}) collective-permute-start(bf16[27,32,512]{2,1,0:T(8,128)(2,1)} %collective-permute-done.25), channel_id=1, source_target_pairs={{0,1},{1,2},{2,3},{3,4},{4,5},{5,6},{6,7},{7,8},{8,9},{9,10},{10,1... | collective-permute-start | bytes 2654216 | tf_op jit(solution)/shard_map/ppermute | solution.py:78
  392.8 30.3 %collective-permute-start.17 = (bf16[3,1,80,512]{3,2,1,0:T(8,128)(2,1)S(1)}, bf16[3,1,80,512]{3,2,1,0:T(8,128)(2,1)S(1)}, u32[]{:S(2)}, u32[]{:S(2)}) collective-permute-start(bf16[3,1,80,512]{3,2,1,0:T(8,128)(2,1)S(1)} %get-tuple-element.14), channel_id=1, source_target_pairs={{0,1},{1,2},{2,3},{3,4},{4,5},{5,6},{6,7},{7,8},{8,9},{9,10},{10,1... | collective-permute-start | bytes 737288 | tf_op jit(solution)/shard_map/ppermute | solution.py:17
  394.1 29.0 %collective-permute-start.18 = (bf16[3,1,80,512]{3,2,1,0:T(8,128)(2,1)S(1)}, bf16[3,1,80,512]{3,2,1,0:T(8,128)(2,1)S(1)}, u32[]{:S(2)}, u32[]{:S(2)}) collective-permute-start(bf16[3,1,80,512]{3,2,1,0:T(8,128)(2,1)S(1)} %get-tuple-element.15), channel_id=1, source_target_pairs={{1,0},{2,1},{3,2},{4,3},{5,4},{6,5},{7,6},{8,7},{9,8},{10,9},{11,1... | collective-permute-start | bytes 737288 | tf_op jit(solution)/shard_map/ppermute | solution.py:19
  (43 other events, 1195.4 us)
